TPU v7x, 128 devices: a whole 4x4x4 slice. The times are simulated.
128 devices in a mesh: dp: 8 (over x, core), eig: 16 (over y, z).
Axes of the slice: x: 4, y: 4, z: 4, core: 2. Of those that a mesh axis runs over, the one named last changes fastest.
Arguments:
- acts: bfloat16 [4096, 8192], P(('dp', 'eig')), may hold values from -6 to 6
- grads: bfloat16 [4096, 8192], P(('dp', 'eig')), may hold values from -6 to 6
- act_basis: bfloat16 [4096, 8192], P('eig'), may hold values from -0.0625 to 0.0625
- grad_basis: bfloat16 [4096, 8192], P('eig'), may hold values from -0.0625 to 0.0625
- eigenvalues: float32 [4096, 4096], P('eig'), may hold values from 0.05 to 20
- query_grads: bfloat16 [32, 256, 4096], P('dp', None, 'eig'), may hold values from -6 to 6
- query_acts: bfloat16 [32, 256, 4096], P('dp'), may hold values from -6 to 6
- cand_local: int32 [8, 16], P('dp'), may hold values from 0 to 7, as said below
- seq_lengths: int32 [8, 8], P('dp'), may hold values from 1 to 128, 512 in all within a row
Outputs:
- scores: float32 [32, 16], P('dp')
Inputs may be any that keep to these rules, and one draw needn't show every extreme that they name: `cand_local`: entry j of an owner's list names a sequence of dp shard j // 2; the 2 entries of one list that name one shard differ. `seq_lengths`: row d lists the lengths of the 8 sequences packed in order in dp shard d's 512 token rows; they sum to 512.
All inputs are finite; a program needn't handle non-finite values.
Results may differ from a plain program's by a relative error of at most 0.006.
Values may be sent and summed in bfloat16 or wider, within the bound.
No kernel may reach another device: no remote copies, remote signals or barrier semaphores. Data moves between devices by JAX's collectives and lax.ppermute only.
A program may use at most 128 MiB of HBM per device.

v0:
```python
import math
import jax
import jax.numpy as jnp
from jax import lax
from jax.sharding import PartitionSpec as P

DAMPING = 0.1


def shards(
    acts,
    grads,
    act_basis,
    grad_basis,
    eigenvalues,
    query_grads,
    query_acts,
    cand_local,
    seq_lengths,
):
    block_width = act_basis.shape[0]
    queries = query_grads.shape[0]
    full_width = query_acts.shape[2]
    seq_count = seq_lengths.shape[1]
    group_rows = acts.shape[0] * lax.axis_size("eig")
    max_len = 2 * group_rows // seq_count
    pick_lists = lax.all_to_all(cand_local, "dp", split_axis=1, concat_axis=0, tiled=True)
    owners = pick_lists.shape[0]
    per_shard = pick_lists.shape[1]
    lengths = seq_lengths[0]
    offsets = jnp.cumsum(lengths) - lengths
    chosen = (
        pick_lists[:, :, None] == jnp.arange(seq_count, dtype=jnp.int32)[None, None, :]
    ).astype(jnp.int32)
    pick_len = jnp.sum(chosen * lengths[None, None, :], axis=2)
    pick_start = jnp.sum(chosen * offsets[None, None, :], axis=2)
    within = jnp.arange(max_len, dtype=jnp.int32)
    is_live = within[None, None, :] < pick_len[:, :, None]
    row_index = jnp.where(is_live, pick_start[:, :, None] + within[None, None, :], -1).reshape(-1)
    select = (row_index[:, None] == jnp.arange(group_rows, dtype=jnp.int32)[None, :]).astype(
        jnp.bfloat16
    )

    def rotate_and_pack(rows, basis):
        shard_rows = lax.all_gather(rows, "eig", axis=0, tiled=True)
        rotated = jnp.dot(shard_rows, basis.T, preferred_element_type=jnp.float32).astype(
            jnp.bfloat16
        )
        rotated = lax.optimization_barrier(rotated)
        packed = jnp.dot(select, rotated, preferred_element_type=jnp.float32).astype(jnp.bfloat16)
        packed = packed.reshape(owners, per_shard * max_len, block_width)
        return lax.all_to_all(packed, "dp", split_axis=0, concat_axis=0, tiled=True)

    act_narrow = rotate_and_pack(acts, act_basis)
    act_recv = lax.all_gather(act_narrow, "eig", axis=2, tiled=True)
    grad_recv = rotate_and_pack(grads, grad_basis)
    slot_count = owners * per_shard * max_len
    grad_flat = grad_recv.reshape(slot_count, block_width).astype(jnp.float32)
    act_flat = act_recv.reshape(slot_count, full_width)
    damped = eigenvalues + DAMPING
    query_outer = jnp.einsum(
        "qti,qtk->qik", query_grads, query_acts, preferred_element_type=jnp.float32
    )
    precond = (query_outer / damped[None]).astype(jnp.bfloat16)
    precond = lax.optimization_barrier(precond.reshape(queries * block_width, full_width))
    projected = lax.dot_general(
        act_flat, precond, (((1,), (1,)), ((), ())), preferred_element_type=jnp.float32
    )
    projected = lax.optimization_barrier(projected).reshape(slot_count, queries, block_width)
    per_token = jnp.sum(projected * grad_flat[:, None, :], axis=2)
    partial_sums = jnp.sum(per_token.reshape(owners * per_shard, max_len, queries), axis=1).T
    summed = lax.psum(partial_sums, "eig")
    score_scale = 1.0 / (full_width * 4.0 * math.sqrt(query_acts.shape[1]))
    return summed * score_scale


def solution(mesh):
    placed = (
        P(("dp", "eig"), None),
        P(("dp", "eig"), None),
        P("eig", None),
        P("eig", None),
        P("eig", None),
        P("dp", None, "eig"),
        P("dp", None, None),
        P("dp", None),
        P("dp", None),
    )
    return jax.shard_map(
        shards, mesh=mesh, in_specs=placed, out_specs=P("dp", None), check_vma=False
    )
```

profile of v0, /device:TPU:0, one launch (start us, length us, event | category | flops | bytes accessed | tf_op | source)
XLA Modules:
  0.0 363.8 jit_solution(16105542730583716110)
XLA Ops:
  6.5 0.0 copy-start
  6.5 0.0 all-gather.4.cloned.1.call-start
  6.5 0.7 all-gather.4.cloned.1.call-update
  7.3 0.0 all-gather.8.cloned.1.call-start
  7.3 0.7 all-gather.8.cloned.1.call-update
  8.0 0.5 broadcast.27
  8.5 1.3 reduce.3
  9.8 0.7 all_to_all.16
  10.5 4.4 %all-to-all-start = ((s32[1,8,2]{2,0,1:T(1,128)}), s32[1,8,2]{2,0,1:T(1,128)S(1)}, u32[]{:S(2)}, u32[]{:S(2)}) async-start(s32[1,8,2]{2,0,1:T(1,128)} %bitcast), calls=%async_computation | async-start | bytes 8192 | tf_op jit(solution)/shard_map/all_to_all | solution.py:27
  14.9 0.0 all-gather.6.cloned.1.call-start
  15.0 0.8 reduce-window.8
  15.8 0.7 bitcast_subtract_fusion
  16.5 3.7 %all-to-all-done = s32[1,8,2]{2,0,1:T(1,128)S(1)} async-done(((s32[1,8,2]{2,0,1:T(1,128)}), s32[1,8,2]{2,0,1:T(1,128)S(1)}, u32[]{:S(2)}, u32[]{:S(2)}) %all-to-all-start) | async-done | bytes 96 | tf_op jit(solution)/shard_map/all_to_all | solution.py:27
  20.2 0.1 copy.26
  20.3 0.9 select_reduce_fusion.1
  21.2 0.1 copy.27
  21.2 0.1 copy.28
  21.3 0.1 compare_select_fusion
  21.4 61.6 %all-gather.4.cloned.1.call-done = bf16[512,8192]{1,0:T(8,128)(2,1)} async-done(((bf16[32,8192]{1,0:T(8,128)(2,1)}), bf16[512,8192]{1,0:T(8,128)(2,1)}) %all-gather.4.cloned.1.call-update) | async-done | bytes 8388624 | tf_op jit(solution)/shard_map/all_gather | solution.py:45
  83.0 6.9 %convolution_convert_fusion.1 = bf16[512,256]{1,0:T(8,128)(2,1)S(1)} fusion(bf16[512,8192]{1,0:T(8,128)(2,1)} %all-gather.4.cloned.1.call-done, bf16[256,8192]{1,0:T(8,128)(2,1)} %param.11), kind=kOutput, calls=%fused_computation.11 | convolution fusion | flops 2147614720 | bytes 12845056 | tf_op jit(solution)/shard_map/dot_general | solution.py:46
  89.9 1.1 fusion.2
  91.0 20.1 %all_to_all.23 = bf16[8,256,256]{2,1,0:T(8,128)(2,1)} all-to-all(bf16[8,256,256]{2,1,0:T(8,128)(2,1)S(1)} %bitcast.28), channel_id=1, replica_groups=mesh['dp'=8,'eig'=16] {'dp'}, dimensions={0} | all-to-all | bytes 2097152 | tf_op jit(solution)/shard_map/all_to_all | solution.py:52
  111.1 0.0 all-gather.6.cloned.1.call-update
  111.2 4.8 %broadcast_add_fusion = f32[256,4096]{1,0:T(8,128)} fusion(f32[256,4096]{1,0:T(8,128)} %param.13), kind=kLoop, calls=%fused_computation.7 | loop fusion | flops 1048576 | bytes 8388608 | tf_op jit(solution)/shard_map/add | solution.py:60
  115.9 39.8 %all-gather.8.cloned.1.call-done = bf16[512,8192]{1,0:T(8,128)(2,1)} async-done(((bf16[32,8192]{1,0:T(8,128)(2,1)}), bf16[512,8192]{1,0:T(8,128)(2,1)}) %all-gather.8.cloned.1.call-update) | async-done | bytes 8388624 | tf_op jit(solution)/shard_map/all_gather | solution.py:45
  155.7 6.9 %convolution_convert_fusion = bf16[512,256]{1,0:T(8,128)(2,1)S(1)} fusion(bf16[512,8192]{1,0:T(8,128)(2,1)} %all-gather.8.cloned.1.call-done, bf16[256,8192]{1,0:T(8,128)(2,1)} %param.12), kind=kOutput, calls=%fused_computation.10 | convolution fusion | flops 2147614720 | bytes 12845056 | tf_op jit(solution)/shard_map/dot_general | solution.py:46
  162.6 1.9 fusion.3
  164.5 4.3 %all-to-all-start.2 = ((bf16[8,256,256]{2,1,0:T(8,128)(2,1)}), bf16[8,256,256]{2,1,0:T(8,128)(2,1)S(1)}, u32[]{:S(2)}, u32[]{:S(2)}) async-start(bf16[8,256,256]{2,1,0:T(8,128)(2,1)} %bitcast.9), calls=%async_computation.2 | async-start | bytes 2097152 | tf_op jit(solution)/shard_map/all_to_all | solution.py:52
  168.7 0.0 copy-done
  168.7 9.2 %divide_convert_fusion = bf16[4,256,4096]{2,1,0:T(8,128)(2,1)} fusion(f32[256,4096]{1,0:T(8,128)} %broadcast_add_fusion, bf16[4,256,256]{2,1,0:T(8,128)(2,1)S(1)} %copy-done, bf16[4,256,4096]{2,1,0:T(8,128)(2,1)} %param.15), kind=kOutput, calls=%fused_computation | convolution fusion | flops 2155872256 | bytes 21495808 | tf_op jit(solution)/shard_map/qti,qtk->qik/dot_general | solution.py:61
  177.9 6.7 %all-to-all-done.2 = bf16[8,256,256]{2,1,0:T(8,128)(2,1)S(1)} async-done(((bf16[8,256,256]{2,1,0:T(8,128)(2,1)}), bf16[8,256,256]{2,1,0:T(8,128)(2,1)S(1)}, u32[]{:S(2)}, u32[]{:S(2)}) %all-to-all-start.2) | async-done | bytes 1048608 | tf_op jit(solution)/shard_map/all_to_all | solution.py:52
  184.7 0.0 copy-start.2
  184.7 1.1 copy-done.2
  185.7 1.4 convert.1
  187.1 90.2 %all-gather.6.cloned.1.call-done = bf16[8,256,4096]{2,1,0:T(8,128)(2,1)} async-done(((bf16[8,256,256]{2,1,0:T(8,128)(2,1)}), bf16[8,256,4096]{2,1,0:T(8,128)(2,1)}) %all-gather.6.cloned.1.call-update) | async-done | bytes 16777232 | tf_op jit(solution)/shard_map/all_gather | solution.py:55
  277.4 24.1 %fusion.6 = f32[2048,1024]{1,0:T(8,128)} fusion(bf16[2048,4096]{1,0:T(8,128)(2,1)} %bitcast.35, bf16[1024,4096]{1,0:T(8,128)(2,1)} %bitcast.36), kind=kOutput, calls=%fused_computation.19 | convolution fusion | flops 17179869184 | bytes 33554432 | tf_op jit(solution)/shard_map/dot_general | solution.py:66
  301.5 0.0 copy-start.1
  301.5 10.6 %reshape.106 = f32[2048,4,256]{2,1,0:T(4,128)} reshape(f32[2048,1024]{1,0:T(8,128)} %fusion.6) | data formatting | bytes 16777216 | tf_op jit(solution)/shard_map/reshape | solution.py:69
  312.1 6.3 %multiply_reduce_fusion = f32[2048,4]{1,0:T(8,128)S(1)} fusion(f32[2048,4,256]{2,1,0:T(4,128)} %reshape.106, f32[2048,256]{1,0:T(8,128)S(1)} %convert.1), kind=kLoop, calls=%fused_computation.1 | loop fusion | flops 4186112 | bytes 10518528 | tf_op jit(solution)/shard_map/reduce_sum | solution.py:70
  318.4 0.1 bitcast_reduce_fusion
  318.5 0.1 copy.32
  318.6 38.1 %psum.7 = f32[4,16]{1,0:T(4,128)S(1)} all-reduce(f32[4,16]{1,0:T(4,128)S(1)} %bitcast.29), channel_id=1, replica_groups=mesh['dp'=8,'eig'=16] {'eig'}, use_global_device_ids=true, to_apply=%region_5.6 | all-reduce | flops 64 | bytes 512 | tf_op jit(solution)/shard_map/psum | solution.py:72
  356.7 0.6 broadcast_multiply_fusion
  357.3 0.0 copy-done.1
Async XLA Ops:
  6.5 162.2 %copy-start = (bf16[4,256,256]{2,1,0:T(8,128)(2,1)S(1)}, bf16[4,256,256]{2,1,0:T(8,128)(2,1)}, u32[]{:S(2)}) copy-start(bf16[4,256,256]{2,1,0:T(8,128)(2,1)} %param.14) | copy-start | bytes 1572868
  6.5 76.4 %all-gather.4.cloned.1.call-start = ((), (), s32[]{:S(2)}) async-start(), calls=%async_computation.3 | async-start | bytes 8912896 | tf_op jit(solution)/shard_map/all_gather | solution.py:45
  7.3 148.4 %all-gather.8.cloned.1.call-start = ((), (), s32[]{:S(2)}) async-start(), calls=%async_computation.5 | async-start | bytes 8912896 | tf_op jit(solution)/shard_map/all_gather | solution.py:45
  10.5 9.7 %all-to-all-start = ((s32[1,8,2]{2,0,1:T(1,128)}), s32[1,8,2]{2,0,1:T(1,128)S(1)}, u32[]{:S(2)}, u32[]{:S(2)}) async-start(s32[1,8,2]{2,0,1:T(1,128)} %bitcast), calls=%async_computation | async-start | bytes 8192 | tf_op jit(solution)/shard_map/all_to_all | solution.py:27
  14.9 262.5 %all-gather.6.cloned.1.call-start = ((), (), s32[]{:S(2)}) async-start(), calls=%async_computation.4 | async-start | bytes 17825792 | tf_op jit(solution)/shard_map/all_gather | solution.py:55
  164.5 20.2 %all-to-all-start.2 = ((bf16[8,256,256]{2,1,0:T(8,128)(2,1)}), bf16[8,256,256]{2,1,0:T(8,128)(2,1)S(1)}, u32[]{:S(2)}, u32[]{:S(2)}) async-start(bf16[8,256,256]{2,1,0:T(8,128)(2,1)} %bitcast.9), calls=%async_computation.2 | async-start | bytes 2097152 | tf_op jit(solution)/shard_map/all_to_all | solution.py:52
  184.7 1.1 copy-start.2
  301.5 55.8 %copy-start.1 = (bf16[4,256,256]{2,1,0:T(8,128)(2,1)S(1)}, bf16[4,256,256]{2,1,0:T(8,128)(2,1)}, u32[]{:S(2)}) copy-start(bf16[4,256,256]{2,1,0:T(8,128)(2,1)} %param.14) | copy-start | bytes 1572868
Sparse Core Ops, SparseCore 0:
  9.5 73.4 all-gather.3
  85.1 70.4 all-gather.7
  157.8 119.5 all-gather.5
where the time goes:
time: 364 us
  waiting for transfers between devices  203 us (56%)
  blocking collectives  58.3 us (16%)
  matrix products  50.1 us (14%)
  other arithmetic  16.9 us (5%)
  local copies, waits for them, and re-layouts  13.2 us (4%)
  between operations  13.2 us (4%)
  starting transfers between devices  8.75 us (2%)
    all_gather x2, waiting for transfers between devices, rotate_and_pack(): shard_rows = lax.all_gather(rows, 'eig', axis=0, tiled=True)  101 us
    all_gather x1, waiting for transfers between devices, shards(): act_recv = lax.all_gather(act_narrow, 'eig', axis=2, tiled=True)  90.2 us
    psum x1, blocking collectives, shards(): summed = lax.psum(partial_sums, 'eig')  38.1 us
    dot_general x1, matrix products, shards(): lax.dot_general(act_flat, precond, (((1,), (1,)), ((), ())), preferred_el...  24.1 us
    all_to_all x1, blocking collectives, rotate_and_pack(): return lax.all_to_all(packed, 'dp', split_axis=0, concat_axis=0, tiled=True)  20.1 us
    dot_general x2, matrix products, rotate_and_pack(): jnp.dot(shard_rows, basis.T, preferred_element_type=jnp.float32)  13.9 us
    reshape x1, local copies, waits for them, and re-layouts, shards(): lax.optimization_barrier(projected)  10.6 us
    dot_general x1, matrix products, shards(): jnp.einsum('qti,qtk->qik', query_grads, query_acts, preferred_element_typ...  9.21 us
  transfers between devices with their start and end apart: 5, of which 5 were waited for; matrix products, arithmetic and copies ran while one was open for 10% of the time, Pallas kernels for 0%

commit v1 on v0

--- a/solution.py
+++ b/solution.py
@@ -52,7 +52,21 @@
         return lax.all_to_all(packed, "dp", split_axis=0, concat_axis=0, tiled=True)
 
     act_narrow = rotate_and_pack(acts, act_basis)
-    act_recv = lax.all_gather(act_narrow, "eig", axis=2, tiled=True)
+    ways, here, lap = (lax.axis_size("eig"), lax.axis_index("eig"), act_narrow.shape[2])
+    lengths_2 = [n * ways if d == 2 else n for d, n in enumerate(act_narrow.shape)]
+    full = lax.dynamic_update_slice_in_dim(
+        jnp.zeros(lengths_2, act_narrow.dtype), act_narrow, here * lap, axis=2
+    )
+    going_up = going_down = act_narrow
+    for far in range(1, ways // 2 + 1):
+        going_up = lax.ppermute(going_up, "eig", [(d, (d + 1) % ways) for d in range(ways)])
+        full = lax.dynamic_update_slice_in_dim(full, going_up, (here - far) % ways * lap, axis=2)
+        if 2 * far < ways:
+            going_down = lax.ppermute(going_down, "eig", [(d, (d - 1) % ways) for d in range(ways)])
+            full = lax.dynamic_update_slice_in_dim(
+                full, going_down, (here + far) % ways * lap, axis=2
+            )
+    act_recv = full
     grad_recv = rotate_and_pack(grads, grad_basis)
     slot_count = owners * per_shard * max_len
     grad_flat = grad_recv.reshape(slot_count, block_width).astype(jnp.float32)

time: 364 us -> 434 us (1.19)
  starting transfers between devices: 8.75 us -> 46.1 us
  local copies, waits for them, and re-layouts: 13.2 us -> 32.2 us
  waiting for transfers between devices: 203 us -> 222 us
    ppermute x0 -> x15, waiting for transfers between devices: none -> 155 us  [the longest x8 141 us: shards(): lax.ppermute(going_up, 'eig', [(d, (d + 1) % ways) for d in range(ways)])]
    all_gather x1 -> x0, waiting for transfers between devices: 90.2 us -> none  [shards(): act_recv = lax.all_gather(act_narrow, 'eig', axis=2, tiled=True)]
    all_gather x2, waiting for transfers between devices: 101 us -> 61.6 us  [rotate_and_pack(): shard_rows = lax.all_gather(rows, 'eig', axis=0, tiled=True)]
    ppermute x0 -> x15, starting transfers between devices: none -> 38 us  [the longest x7 36.5 us: shards(): lax.ppermute(going_down, 'eig', [(d, (d - 1) % ways) for d in range(ways)])]
    dynamic_update_slice x0 -> x16, local copies, waits for them, and re-layouts: none -> 17 us  [the longest x8 8.49 us: shards(): lax.dynamic_update_slice_in_dim(full, going_up, (here - far) % ways * lap...]
    all_to_all x1, waiting for transfers between devices: 6.71 us -> 0.01 us  [rotate_and_pack(): return lax.all_to_all(packed, 'dp', split_axis=0, concat_axis=0, tiled=True)]
  transfers between devices with their start and end apart: 5 -> 19, of which waited for: 5 -> 11; matrix products, arithmetic and copies ran while one was open for 10% -> 12% of each run, Pallas kernels for 0% -> 0%
where the time goes in v1:
time: 434 us; the launch traced here: 433 us
  waiting for transfers between devices  222 us (51%)
  blocking collectives  55.6 us (13%)
  matrix products  49.5 us (11%)
  starting transfers between devices  46.1 us (11%)
  local copies, waits for them, and re-layouts  32.2 us (7%)
  other arithmetic  14.6 us (3%)
  between operations  13.7 us (3%)
    ppermute x8, waiting for transfers between devices, shards(): lax.ppermute(going_up, 'eig', [(d, (d + 1) % ways) for d in range(ways)])  141 us
    all_gather x2, waiting for transfers between devices, rotate_and_pack(): shard_rows = lax.all_gather(rows, 'eig', axis=0, tiled=True)  61.6 us
    ppermute x7, starting transfers between devices, shards(): lax.ppermute(going_down, 'eig', [(d, (d - 1) % ways) for d in range(ways)])  36.5 us
    psum x1, blocking collectives, shards(): summed = lax.psum(partial_sums, 'eig')  35.4 us
    dot_general x1, matrix products, shards(): lax.dot_general(act_flat, precond, (((1,), (1,)), ((), ())), preferred_el...  23.5 us
    all_to_all x1, blocking collectives, rotate_and_pack(): return lax.all_to_all(packed, 'dp', split_axis=0, concat_axis=0, tiled=True)  20.1 us
    dot_general x2, matrix products, rotate_and_pack(): jnp.dot(shard_rows, basis.T, preferred_element_type=jnp.float32)  14 us
    ppermute x7, waiting for transfers between devices, shards(): lax.ppermute(going_down, 'eig', [(d, (d - 1) % ways) for d in range(ways)])  13.7 us
  transfers between devices with their start and end apart: 19, of which 11 were waited for; matrix products, arithmetic and copies ran while one was open for 12% of the time, Pallas kernels for 0%

profile of v1, /device:TPU:0, one launch (start us, length us, event | category | flops | bytes accessed | tf_op | source)
XLA Modules:
  0.0 433.5 jit_solution(8152148257108456582)
XLA Ops:
  6.5 0.7 all-gather.3.cloned.1.call-update
  7.3 0.7 all-gather.5.cloned.1.call-update
  8.0 0.5 broadcast.42
  8.5 1.3 reduce.3
  9.8 0.7 all_to_all.16
  10.5 4.4 %all-to-all-start = ((s32[1,8,2]{2,0,1:T(1,128)}), s32[1,8,2]{2,0,1:T(1,128)S(1)}, u32[]{:S(2)}, u32[]{:S(2)}) async-start(s32[1,8,2]{2,0,1:T(1,128)} %bitcast), calls=%async_computation | async-start | bytes 8192 | tf_op jit(solution)/shard_map/all_to_all | solution.py:27
  14.9 0.8 reduce-window.8
  15.8 0.7 bitcast_subtract_fusion
  16.4 3.8 all-to-all-done
  20.3 0.9 select_reduce_fusion.1
  21.2 0.1 copy.27
  21.2 0.1 copy.28
  21.3 0.1 compare_select_fusion
  21.4 61.6 %all-gather.3.cloned.1.call-done = bf16[512,8192]{1,0:T(8,128)(2,1)} async-done(((bf16[32,8192]{1,0:T(8,128)(2,1)}), bf16[512,8192]{1,0:T(8,128)(2,1)}) %all-gather.3.cloned.1.call-update) | async-done | bytes 8388624 | tf_op jit(solution)/shard_map/all_gather | solution.py:45
  83.0 7.1 %convolution_convert_fusion.1 = bf16[512,256]{1,0:T(8,128)(2,1)S(1)} fusion(bf16[512,8192]{1,0:T(8,128)(2,1)} %all-gather.3.cloned.1.call-done, bf16[256,8192]{1,0:T(8,128)(2,1)} %param.11), kind=kOutput, calls=%fused_computation.11 | convolution fusion | flops 2147614720 | bytes 12845056 | tf_op jit(solution)/shard_map/dot_general | solution.py:46
  90.1 1.1 fusion.2
  91.2 20.1 %all_to_all.23 = bf16[8,256,256]{2,1,0:T(8,128)(2,1)} all-to-all(bf16[8,256,256]{2,1,0:T(8,128)(2,1)S(1)} %bitcast.30), channel_id=1, replica_groups=mesh['dp'=8,'eig'=16] {'dp'}, dimensions={0} | all-to-all | bytes 2097152 | tf_op jit(solution)/shard_map/all_to_all | solution.py:52
  111.3 1.3 collective-permute-start
  112.6 4.0 collective-permute-start.1
  116.6 39.8 %collective-permute-done = bf16[8,256,256]{2,1,0:T(8,128)(2,1)S(1)} collective-permute-done((bf16[8,256,256]{2,1,0:T(8,128)(2,1)}, bf16[8,256,256]{2,1,0:T(8,128)(2,1)S(1)}, u32[]{:S(2)}, u32[]{:S(2)}) %collective-permute-start) | collective-permute-done | bytes 1048608 | tf_op jit(solution)/shard_map/ppermute | solution.py:62
  156.5 1.0 copy-done.4
  157.5 3.6 collective-permute-done.1
  161.1 5.7 %collective-permute-start.3 = (bf16[8,256,256]{2,1,0:T(8,128)(2,1)S(1)}, bf16[8,256,256]{2,1,0:T(8,128)(2,1)S(1)}, u32[]{:S(2)}, u32[]{:S(2)}) collective-permute-start(bf16[8,256,256]{2,1,0:T(8,128)(2,1)S(1)} %collective-permute-done.1), channel_id=1, source_target_pairs={{0,15},{1,0},{2,1},{3,2},{4,3},{5,4},{6,5},{7,6},{8,7},{9,8},{10,9... | collective-permute-start | bytes 3145736 | tf_op jit(solution)/shard_map/ppermute | solution.py:65
  166.8 28.7 %collective-permute-done.2 = bf16[8,256,256]{2,1,0:T(8,128)(2,1)S(1)} collective-permute-done((bf16[8,256,256]{2,1,0:T(8,128)(2,1)S(1)}, bf16[8,256,256]{2,1,0:T(8,128)(2,1)S(1)}, u32[]{:S(2)}, u32[]{:S(2)}) %collective-permute-start.2) | collective-permute-done | bytes 1048608 | tf_op jit(solution)/shard_map/ppermute | solution.py:62
  195.6 5.3 %collective-permute-start.5 = (bf16[8,256,256]{2,1,0:T(8,128)(2,1)S(1)}, bf16[8,256,256]{2,1,0:T(8,128)(2,1)S(1)}, u32[]{:S(2)}, u32[]{:S(2)}) collective-permute-start(bf16[8,256,256]{2,1,0:T(8,128)(2,1)S(1)} %collective-permute-done.3), channel_id=1, source_target_pairs={{0,15},{1,0},{2,1},{3,2},{4,3},{5,4},{6,5},{7,6},{8,7},{9,8},{10,9... | collective-permute-start | bytes 3145736 | tf_op jit(solution)/shard_map/ppermute | solution.py:65
  200.9 21.4 %collective-permute-done.4 = bf16[8,256,256]{2,1,0:T(8,128)(2,1)S(1)} collective-permute-done((bf16[8,256,256]{2,1,0:T(8,128)(2,1)S(1)}, bf16[8,256,256]{2,1,0:T(8,128)(2,1)S(1)}, u32[]{:S(2)}, u32[]{:S(2)}) %collective-permute-start.4) | collective-permute-done | bytes 1048608 | tf_op jit(solution)/shard_map/ppermute | solution.py:62
  222.3 5.3 %collective-permute-start.7 = (bf16[8,256,256]{2,1,0:T(8,128)(2,1)S(1)}, bf16[8,256,256]{2,1,0:T(8,128)(2,1)S(1)}, u32[]{:S(2)}, u32[]{:S(2)}) collective-permute-start(bf16[8,256,256]{2,1,0:T(8,128)(2,1)S(1)} %collective-permute-done.5), channel_id=1, source_target_pairs={{0,15},{1,0},{2,1},{3,2},{4,3},{5,4},{6,5},{7,6},{8,7},{9,8},{10,9... | collective-permute-start | bytes 3145736 | tf_op jit(solution)/shard_map/ppermute | solution.py:65
  227.6 20.5 %collective-permute-done.6 = bf16[8,256,256]{2,1,0:T(8,128)(2,1)S(1)} collective-permute-done((bf16[8,256,256]{2,1,0:T(8,128)(2,1)S(1)}, bf16[8,256,256]{2,1,0:T(8,128)(2,1)S(1)}, u32[]{:S(2)}, u32[]{:S(2)}) %collective-permute-start.6) | collective-permute-done | bytes 1048608 | tf_op jit(solution)/shard_map/ppermute | solution.py:62
  248.3 2.3 broadcast_add_fusion
  250.6 5.4 %collective-permute-start.9 = (bf16[8,256,256]{2,1,0:T(8,128)(2,1)S(1)}, bf16[8,256,256]{2,1,0:T(8,128)(2,1)}, u32[]{:S(2)}, u32[]{:S(2)}) collective-permute-start(bf16[8,256,256]{2,1,0:T(8,128)(2,1)S(1)} %collective-permute-done.7), channel_id=1, source_target_pairs={{0,15},{1,0},{2,1},{3,2},{4,3},{5,4},{6,5},{7,6},{8,7},{9,8},{10,9... | collective-permute-start | bytes 3145736 | tf_op jit(solution)/shard_map/ppermute | solution.py:65
  256.0 17.4 %collective-permute-done.8 = bf16[8,256,256]{2,1,0:T(8,128)(2,1)} collective-permute-done((bf16[8,256,256]{2,1,0:T(8,128)(2,1)S(1)}, bf16[8,256,256]{2,1,0:T(8,128)(2,1)}, u32[]{:S(2)}, u32[]{:S(2)}) %collective-permute-start.8) | collective-permute-done | bytes 1048608 | tf_op jit(solution)/shard_map/ppermute | solution.py:62
  273.5 6.9 %convolution_convert_fusion = bf16[512,256]{1,0:T(8,128)(2,1)S(1)} fusion(bf16[512,8192]{1,0:T(8,128)(2,1)} %all-gather.5.cloned.1.call-done, bf16[256,8192]{1,0:T(8,128)(2,1)} %param.12), kind=kOutput, calls=%fused_computation.10 | convolution fusion | flops 2147614720 | bytes 12845056 | tf_op jit(solution)/shard_map/dot_general | solution.py:46
  280.4 1.9 fusion.3
  282.3 3.6 all-to-all-start.2
  285.9 5.4 %collective-permute-start.11 = (bf16[8,256,256]{2,1,0:T(8,128)(2,1)}, bf16[8,256,256]{2,1,0:T(8,128)(2,1)}, u32[]{:S(2)}, u32[]{:S(2)}) collective-permute-start(bf16[8,256,256]{2,1,0:T(8,128)(2,1)} %collective-permute-done.9), channel_id=1, source_target_pairs={{0,15},{1,0},{2,1},{3,2},{4,3},{5,4},{6,5},{7,6},{8,7},{9,8},{10,9... | collective-permute-start | bytes 3145736 | tf_op jit(solution)/shard_map/ppermute | solution.py:65
  291.3 6.7 %collective-permute-done.10 = bf16[8,256,256]{2,1,0:T(8,128)(2,1)} collective-permute-done((bf16[8,256,256]{2,1,0:T(8,128)(2,1)}, bf16[8,256,256]{2,1,0:T(8,128)(2,1)}, u32[]{:S(2)}, u32[]{:S(2)}) %collective-permute-start.10) | collective-permute-done | bytes 1048608 | tf_op jit(solution)/shard_map/ppermute | solution.py:62
  297.9 9.1 %divide_convert_fusion = bf16[4,256,4096]{2,1,0:T(8,128)(2,1)} fusion(f32[256,4096]{1,0:T(8,128)} %broadcast_add_fusion, bf16[4,256,256]{2,1,0:T(8,128)(2,1)S(1)} %copy-done, bf16[4,256,4096]{2,1,0:T(8,128)(2,1)} %param.15), kind=kOutput, calls=%fused_computation | convolution fusion | flops 2155872256 | bytes 21495808 | tf_op jit(solution)/shard_map/qti,qtk->qik/dot_general | solution.py:75
  307.0 1.5 convert.1
  308.5 1.9 broadcast_in_dim.5
  310.4 1.4 constant_dynamic-update-slice_fusion.15
  311.8 1.4 constant_dynamic-update-slice_fusion.14
  313.2 1.4 constant_dynamic-update-slice_fusion.13
  314.6 1.4 constant_dynamic-update-slice_fusion.12
  315.9 1.4 constant_dynamic-update-slice_fusion.11
  317.3 1.4 constant_dynamic-update-slice_fusion.10
  318.7 5.4 %collective-permute-start.13 = (bf16[8,256,256]{2,1,0:T(8,128)(2,1)}, bf16[8,256,256]{2,1,0:T(8,128)(2,1)S(1)}, u32[]{:S(2)}, u32[]{:S(2)}) collective-permute-start(bf16[8,256,256]{2,1,0:T(8,128)(2,1)} %collective-permute-done.11), channel_id=1, source_target_pairs={{0,15},{1,0},{2,1},{3,2},{4,3},{5,4},{6,5},{7,6},{8,7},{9,8},{10,9... | collective-permute-start | bytes 3145736 | tf_op jit(solution)/shard_map/ppermute | solution.py:65
  324.1 1.4 constant_dynamic-update-slice_fusion.9
  325.6 0.1 constant_dynamic-update-slice_fusion.8
  325.7 0.1 constant_dynamic-update-slice_fusion.7
  325.9 1.4 constant_dynamic-update-slice_fusion.6
  327.3 1.4 constant_dynamic-update-slice_fusion.5
  328.6 1.4 constant_dynamic-update-slice_fusion.4
  330.0 1.4 constant_dynamic-update-slice_fusion.3
  331.4 1.4 constant_dynamic-update-slice_fusion.2
  332.8 10.1 %collective-permute-done.13 = bf16[8,256,256]{2,1,0:T(8,128)(2,1)S(1)} collective-permute-done((bf16[8,256,256]{2,1,0:T(8,128)(2,1)}, bf16[8,256,256]{2,1,0:T(8,128)(2,1)S(1)}, u32[]{:S(2)}, u32[]{:S(2)}) %collective-permute-start.13) | collective-permute-done | bytes 1048608 | tf_op jit(solution)/shard_map/ppermute | solution.py:65
  342.9 0.1 constant_dynamic-update-slice_fusion.1
  343.0 6.7 %collective-permute-done.14 = bf16[8,256,256]{2,1,0:T(8,128)(2,1)S(1)} collective-permute-done((bf16[8,256,256]{2,1,0:T(8,128)(2,1)}, bf16[8,256,256]{2,1,0:T(8,128)(2,1)S(1)}, u32[]{:S(2)}, u32[]{:S(2)}) %collective-permute-start.14) | collective-permute-done | bytes 1048608 | tf_op jit(solution)/shard_map/ppermute | solution.py:62
  349.7 0.1 constant_dynamic-update-slice_fusion
  349.9 23.5 %fusion.6 = f32[2048,1024]{1,0:T(8,128)} fusion(bf16[2048,4096]{1,0:T(8,128)(2,1)S(1)} %bitcast.27, bf16[1024,4096]{1,0:T(8,128)(2,1)} %bitcast.37), kind=kOutput, calls=%fused_computation.35 | convolution fusion | flops 17179869184 | bytes 33554432 | tf_op jit(solution)/shard_map/dot_general | solution.py:80
  373.4 10.8 %reshape.106 = f32[2048,4,256]{2,1,0:T(4,128)} reshape(f32[2048,1024]{1,0:T(8,128)} %fusion.6) | data formatting | bytes 16777216 | tf_op jit(solution)/shard_map/reshape | solution.py:83
  384.2 6.3 %multiply_reduce_fusion = f32[2048,4]{1,0:T(8,128)S(1)} fusion(f32[2048,4,256]{2,1,0:T(4,128)} %reshape.106, f32[2048,256]{1,0:T(8,128)S(1)} %copy-done.2), kind=kLoop, calls=%fused_computation.1 | loop fusion | flops 4186112 | bytes 10518528 | tf_op jit(solution)/shard_map/reduce_sum | solution.py:84
  390.5 0.1 bitcast_reduce_fusion
  390.6 35.4 %psum.7 = f32[4,16]{1,0:T(4,128)S(1)} all-reduce(f32[4,16]{1,0:T(4,128)S(1)} %bitcast.31), channel_id=1, replica_groups=mesh['dp'=8,'eig'=16] {'eig'}, use_global_device_ids=true, to_apply=%region_5.6 | all-reduce | flops 64 | bytes 512 | tf_op jit(solution)/shard_map/psum | solution.py:86
  426.1 0.6 broadcast_multiply_fusion
  (46 shorter events, 0.5 us)
Async XLA Ops:
  6.5 291.4 %copy-start = (bf16[4,256,256]{2,1,0:T(8,128)(2,1)S(1)}, bf16[4,256,256]{2,1,0:T(8,128)(2,1)}, u32[]{:S(2)}) copy-start(bf16[4,256,256]{2,1,0:T(8,128)(2,1)} %param.14) | copy-start | bytes 1572868
  6.5 76.4 %all-gather.3.cloned.1.call-start = ((), (), s32[]{:S(2)}) async-start(), calls=%async_computation.3 | async-start | bytes 8912896 | tf_op jit(solution)/shard_map/all_gather | solution.py:45
  7.3 266.2 %all-gather.5.cloned.1.call-start = ((), (), s32[]{:S(2)}) async-start(), calls=%async_computation.4 | async-start | bytes 8912896 | tf_op jit(solution)/shard_map/all_gather | solution.py:45
  10.5 9.7 %all-to-all-start = ((s32[1,8,2]{2,0,1:T(1,128)}), s32[1,8,2]{2,0,1:T(1,128)S(1)}, u32[]{:S(2)}, u32[]{:S(2)}) async-start(s32[1,8,2]{2,0,1:T(1,128)} %bitcast), calls=%async_computation | async-start | bytes 8192 | tf_op jit(solution)/shard_map/all_to_all | solution.py:27
  83.0 165.3 %copy-start.3 = (f32[256,4096]{1,0:T(8,128)S(1)}, f32[256,4096]{1,0:T(8,128)}, u32[]{:S(2)}) copy-start(f32[256,4096]{1,0:T(8,128)} %param.13) | copy-start | bytes 12582916
  111.3 45.2 %collective-permute-start = (bf16[8,256,256]{2,1,0:T(8,128)(2,1)}, bf16[8,256,256]{2,1,0:T(8,128)(2,1)S(1)}, u32[]{:S(2)}, u32[]{:S(2)}) collective-permute-start(bf16[8,256,256]{2,1,0:T(8,128)(2,1)} %all_to_all.23), channel_id=1, source_target_pairs={{0,1},{1,2},{2,3},{3,4},{4,5},{5,6},{6,7},{7,8},{8,9},{9,10},{10,1... | collective-permute-start | bytes 3145736 | tf_op jit(solution)/shard_map/ppermute | solution.py:62
  112.6 48.4 %collective-permute-start.1 = (bf16[8,256,256]{2,1,0:T(8,128)(2,1)}, bf16[8,256,256]{2,1,0:T(8,128)(2,1)S(1)}, u32[]{:S(2)}, u32[]{:S(2)}) collective-permute-start(bf16[8,256,256]{2,1,0:T(8,128)(2,1)} %all_to_all.23), channel_id=1, source_target_pairs={{0,15},{1,0},{2,1},{3,2},{4,3},{5,4},{6,5},{7,6},{8,7},{9,8},{10,9... | collective-permute-start | bytes 3145736 | tf_op jit(solution)/shard_map/ppermute | solution.py:65
  156.5 1.0 copy-start.4
  157.5 38.1 %collective-permute-start.2 = (bf16[8,256,256]{2,1,0:T(8,128)(2,1)S(1)}, bf16[8,256,256]{2,1,0:T(8,128)(2,1)S(1)}, u32[]{:S(2)}, u32[]{:S(2)}) collective-permute-start(bf16[8,256,256]{2,1,0:T(8,128)(2,1)S(1)} %collective-permute-done), channel_id=1, source_target_pairs={{0,1},{1,2},{2,3},{3,4},{4,5},{5,6},{6,7},{7,8},{8,9},{9,10},{10,1... | collective-permute-start | bytes 3145736 | tf_op jit(solution)/shard_map/ppermute | solution.py:62
  161.1 34.4 %copy-start.5 = (bf16[8,256,256]{2,1,0:T(8,128)(2,1)}, bf16[8,256,256]{2,1,0:T(8,128)(2,1)S(1)}, u32[]{:S(2)}) copy-start(bf16[8,256,256]{2,1,0:T(8,128)(2,1)S(1)} %collective-permute-done.1) | copy-start | bytes 3145732
  161.1 34.5 %collective-permute-start.3 = (bf16[8,256,256]{2,1,0:T(8,128)(2,1)S(1)}, bf16[8,256,256]{2,1,0:T(8,128)(2,1)S(1)}, u32[]{:S(2)}, u32[]{:S(2)}) collective-permute-start(bf16[8,256,256]{2,1,0:T(8,128)(2,1)S(1)} %collective-permute-done.1), channel_id=1, source_target_pairs={{0,15},{1,0},{2,1},{3,2},{4,3},{5,4},{6,5},{7,6},{8,7},{9,8},{10,9... | collective-permute-start | bytes 3145736 | tf_op jit(solution)/shard_map/ppermute | solution.py:65
  195.5 52.7 %copy-start.8 = (bf16[8,256,256]{2,1,0:T(8,128)(2,1)}, bf16[8,256,256]{2,1,0:T(8,128)(2,1)S(1)}, u32[]{:S(2)}) copy-start(bf16[8,256,256]{2,1,0:T(8,128)(2,1)S(1)} %collective-permute-done.2) | copy-start | bytes 3145732
  195.5 26.8 %collective-permute-start.4 = (bf16[8,256,256]{2,1,0:T(8,128)(2,1)S(1)}, bf16[8,256,256]{2,1,0:T(8,128)(2,1)S(1)}, u32[]{:S(2)}, u32[]{:S(2)}) collective-permute-start(bf16[8,256,256]{2,1,0:T(8,128)(2,1)S(1)} %collective-permute-done.2), channel_id=1, source_target_pairs={{0,1},{1,2},{2,3},{3,4},{4,5},{5,6},{6,7},{7,8},{8,9},{9,10},{10,1... | collective-permute-start | bytes 3145736 | tf_op jit(solution)/shard_map/ppermute | solution.py:62
  195.6 77.9 %copy-start.12 = (bf16[8,256,256]{2,1,0:T(8,128)(2,1)}, bf16[8,256,256]{2,1,0:T(8,128)(2,1)S(1)}, u32[]{:S(2)}) copy-start(bf16[8,256,256]{2,1,0:T(8,128)(2,1)S(1)} %collective-permute-done.3) | copy-start | bytes 3145732
  195.6 26.7 %collective-permute-start.5 = (bf16[8,256,256]{2,1,0:T(8,128)(2,1)S(1)}, bf16[8,256,256]{2,1,0:T(8,128)(2,1)S(1)}, u32[]{:S(2)}, u32[]{:S(2)}) collective-permute-start(bf16[8,256,256]{2,1,0:T(8,128)(2,1)S(1)} %collective-permute-done.3), channel_id=1, source_target_pairs={{0,15},{1,0},{2,1},{3,2},{4,3},{5,4},{6,5},{7,6},{8,7},{9,8},{10,9... | collective-permute-start | bytes 3145736 | tf_op jit(solution)/shard_map/ppermute | solution.py:65
  222.3 25.9 %copy-start.13 = (bf16[8,256,256]{2,1,0:T(8,128)(2,1)}, bf16[8,256,256]{2,1,0:T(8,128)(2,1)S(1)}, u32[]{:S(2)}) copy-start(bf16[8,256,256]{2,1,0:T(8,128)(2,1)S(1)} %collective-permute-done.4) | copy-start | bytes 3145732
  222.3 25.9 %collective-permute-start.6 = (bf16[8,256,256]{2,1,0:T(8,128)(2,1)S(1)}, bf16[8,256,256]{2,1,0:T(8,128)(2,1)S(1)}, u32[]{:S(2)}, u32[]{:S(2)}) collective-permute-start(bf16[8,256,256]{2,1,0:T(8,128)(2,1)S(1)} %collective-permute-done.4), channel_id=1, source_target_pairs={{0,1},{1,2},{2,3},{3,4},{4,5},{5,6},{6,7},{7,8},{8,9},{9,10},{10,1... | collective-permute-start | bytes 3145736 | tf_op jit(solution)/shard_map/ppermute | solution.py:62
  222.3 51.1 %copy-start.11 = (bf16[8,256,256]{2,1,0:T(8,128)(2,1)}, bf16[8,256,256]{2,1,0:T(8,128)(2,1)S(1)}, u32[]{:S(2)}) copy-start(bf16[8,256,256]{2,1,0:T(8,128)(2,1)S(1)} %collective-permute-done.5) | copy-start | bytes 3145732
  222.3 28.3 %collective-permute-start.7 = (bf16[8,256,256]{2,1,0:T(8,128)(2,1)S(1)}, bf16[8,256,256]{2,1,0:T(8,128)(2,1)S(1)}, u32[]{:S(2)}, u32[]{:S(2)}) collective-permute-start(bf16[8,256,256]{2,1,0:T(8,128)(2,1)S(1)} %collective-permute-done.5), channel_id=1, source_target_pairs={{0,15},{1,0},{2,1},{3,2},{4,3},{5,4},{6,5},{7,6},{8,7},{9,8},{10,9... | collective-permute-start | bytes 3145736 | tf_op jit(solution)/shard_map/ppermute | solution.py:65
  248.2 2.4 copy-start.6
  248.2 25.2 %collective-permute-start.8 = (bf16[8,256,256]{2,1,0:T(8,128)(2,1)S(1)}, bf16[8,256,256]{2,1,0:T(8,128)(2,1)}, u32[]{:S(2)}, u32[]{:S(2)}) collective-permute-start(bf16[8,256,256]{2,1,0:T(8,128)(2,1)S(1)} %collective-permute-done.6), channel_id=1, source_target_pairs={{0,1},{1,2},{2,3},{3,4},{4,5},{5,6},{6,7},{7,8},{8,9},{9,10},{10,1... | collective-permute-start | bytes 3145736 | tf_op jit(solution)/shard_map/ppermute | solution.py:62
  250.6 56.4 %copy-start.9 = (bf16[8,256,256]{2,1,0:T(8,128)(2,1)}, bf16[8,256,256]{2,1,0:T(8,128)(2,1)S(1)}, u32[]{:S(2)}) copy-start(bf16[8,256,256]{2,1,0:T(8,128)(2,1)S(1)} %collective-permute-done.7) | copy-start | bytes 3145732
  250.6 35.2 %collective-permute-start.9 = (bf16[8,256,256]{2,1,0:T(8,128)(2,1)S(1)}, bf16[8,256,256]{2,1,0:T(8,128)(2,1)}, u32[]{:S(2)}, u32[]{:S(2)}) collective-permute-start(bf16[8,256,256]{2,1,0:T(8,128)(2,1)S(1)} %collective-permute-done.7), channel_id=1, source_target_pairs={{0,15},{1,0},{2,1},{3,2},{4,3},{5,4},{6,5},{7,6},{8,7},{9,8},{10,9... | collective-permute-start | bytes 3145736 | tf_op jit(solution)/shard_map/ppermute | solution.py:65
  273.4 24.5 %collective-permute-start.10 = (bf16[8,256,256]{2,1,0:T(8,128)(2,1)}, bf16[8,256,256]{2,1,0:T(8,128)(2,1)}, u32[]{:S(2)}, u32[]{:S(2)}) collective-permute-start(bf16[8,256,256]{2,1,0:T(8,128)(2,1)} %collective-permute-done.8), channel_id=1, source_target_pairs={{0,1},{1,2},{2,3},{3,4},{4,5},{5,6},{6,7},{7,8},{8,9},{9,10},{10,1... | collective-permute-start | bytes 3145736 | tf_op jit(solution)/shard_map/ppermute | solution.py:62
  282.3 24.7 %all-to-all-start.2 = ((bf16[8,256,256]{2,1,0:T(8,128)(2,1)}), bf16[8,256,256]{2,1,0:T(8,128)(2,1)S(1)}, u32[]{:S(2)}, u32[]{:S(2)}) async-start(bf16[8,256,256]{2,1,0:T(8,128)(2,1)} %bitcast.29), calls=%async_computation.2 | async-start | bytes 2097152 | tf_op jit(solution)/shard_map/all_to_all | solution.py:52
  285.9 32.8 %collective-permute-start.11 = (bf16[8,256,256]{2,1,0:T(8,128)(2,1)}, bf16[8,256,256]{2,1,0:T(8,128)(2,1)}, u32[]{:S(2)}, u32[]{:S(2)}) collective-permute-start(bf16[8,256,256]{2,1,0:T(8,128)(2,1)} %collective-permute-done.9), channel_id=1, source_target_pairs={{0,15},{1,0},{2,1},{3,2},{4,3},{5,4},{6,5},{7,6},{8,7},{9,8},{10,9... | collective-permute-start | bytes 3145736 | tf_op jit(solution)/shard_map/ppermute | solution.py:65
  297.9 27.5 %collective-permute-start.12 = (bf16[8,256,256]{2,1,0:T(8,128)(2,1)}, bf16[8,256,256]{2,1,0:T(8,128)(2,1)}, u32[]{:S(2)}, u32[]{:S(2)}) collective-permute-start(bf16[8,256,256]{2,1,0:T(8,128)(2,1)} %collective-permute-done.10), channel_id=1, source_target_pairs={{0,1},{1,2},{2,3},{3,4},{4,5},{5,6},{6,7},{7,8},{8,9},{9,10},{10,1... | collective-permute-start | bytes 3145736 | tf_op jit(solution)/shard_map/ppermute | solution.py:62
  307.0 18.6 %copy-start.7 = (bf16[8,256,256]{2,1,0:T(8,128)(2,1)S(1)}, bf16[8,256,256]{2,1,0:T(8,128)(2,1)}, u32[]{:S(2)}) copy-start(bf16[8,256,256]{2,1,0:T(8,128)(2,1)} %copy-done.6) | copy-start | bytes 3145732
  308.5 17.2 %copy-start.10 = (bf16[8,256,256]{2,1,0:T(8,128)(2,1)S(1)}, bf16[8,256,256]{2,1,0:T(8,128)(2,1)}, u32[]{:S(2)}) copy-start(bf16[8,256,256]{2,1,0:T(8,128)(2,1)} %copy-done.9) | copy-start | bytes 3145732
  318.7 24.2 %collective-permute-start.13 = (bf16[8,256,256]{2,1,0:T(8,128)(2,1)}, bf16[8,256,256]{2,1,0:T(8,128)(2,1)S(1)}, u32[]{:S(2)}, u32[]{:S(2)}) collective-permute-start(bf16[8,256,256]{2,1,0:T(8,128)(2,1)} %collective-permute-done.11), channel_id=1, source_target_pairs={{0,15},{1,0},{2,1},{3,2},{4,3},{5,4},{6,5},{7,6},{8,7},{9,8},{10,9... | collective-permute-start | bytes 3145736 | tf_op jit(solution)/shard_map/ppermute | solution.py:65
  325.5 24.3 %collective-permute-start.14 = (bf16[8,256,256]{2,1,0:T(8,128)(2,1)}, bf16[8,256,256]{2,1,0:T(8,128)(2,1)S(1)}, u32[]{:S(2)}, u32[]{:S(2)}) collective-permute-start(bf16[8,256,256]{2,1,0:T(8,128)(2,1)} %collective-permute-done.12), channel_id=1, source_target_pairs={{0,1},{1,2},{2,3},{3,4},{4,5},{5,6},{6,7},{7,8},{8,9},{9,10},{10,1... | collective-permute-start | bytes 3145736 | tf_op jit(solution)/shard_map/ppermute | solution.py:62
  349.9 76.8 %copy-start.1 = (bf16[4,256,256]{2,1,0:T(8,128)(2,1)S(1)}, bf16[4,256,256]{2,1,0:T(8,128)(2,1)}, u32[]{:S(2)}) copy-start(bf16[4,256,256]{2,1,0:T(8,128)(2,1)} %param.14) | copy-start | bytes 1572868
  373.4 10.8 %copy-start.2 = (f32[2048,256]{1,0:T(8,128)S(1)}, f32[2048,256]{1,0:T(8,128)}, u32[]{:S(2)}) copy-start(f32[2048,256]{1,0:T(8,128)} %convert.1) | copy-start | bytes 6291460
Sparse Core Ops, SparseCore 0:
  9.5 73.4 all-gather.2
  85.1 100.6 all-gather.4
